TPU v7x, 128 devices: a whole 4x4x4 slice. The times are simulated.
128 devices in a mesh: row: 8 (over z, core), col: 16 (over x, y).
Axes of the slice: x: 4, y: 4, z: 4, core: 2. Of those that a mesh axis runs over, the one named last changes fastest.
Arguments:
- updates: float32 [16384, 8192], P('col', 'row'), may hold values from -6 to 6
- block_map: int32 [2, 64], replicated, may hold values from 0 to 79, as said below
- own_diag: float32 [10240], P('row'), may hold values from 2 to 6
- panel_inverse: float32 [512, 512], replicated, as said below
Outputs:
- factor_panel: float32 [10240, 512], P('row')
- trailing: float32 [10240, 10240], P('row', 'col')
Inputs may be any that keep to these rules, and one draw needn't show every extreme that they name: `block_map`: within one child the 64 entries name distinct front blocks. Take the child blocks (a, b) held by one device in updates, and the front blocks held by one device in trailing: either exactly 1 of the former land in the latter, or none do. `panel_inverse`: lower triangular with a positive diagonal.
All inputs are finite; a program needn't handle non-finite values.
Results may differ from a plain program's by a relative error of at most 0.000075.
Values sent between devices are 32-bit elements; how exact they have to be, the bound alone decides.
No kernel may reach another device: no remote copies, remote signals or barrier semaphores. Data moves between devices by JAX's collectives and lax.ppermute only.
A program may use at most 128 MiB of HBM per device.

v0:
```python
import jax
import jax.numpy as jnp
from jax import lax
from jax.sharding import PartitionSpec as P

F = 10240
M = 8192
BLK = 128
PANEL = 512


def on_device(updates, block_map, own_diag, panel_inverse):
    row_count = lax.axis_size("row")
    col_count = lax.axis_size("col")
    row_index = lax.axis_index("row")
    col_index = lax.axis_index("col")
    devices_all = row_count * col_count
    local_rows, local_cols = updates.shape
    row_items = local_rows // BLK
    col_items = local_cols // BLK
    half_cols = col_count // 2
    front_blocks = F // BLK
    front_rows = front_blocks // row_count
    front_cols = front_blocks // col_count
    height = front_rows * BLK
    col_width = front_cols * BLK
    block_map = block_map.astype(jnp.int32)
    child = col_index // half_cols
    child_map = jnp.take(block_map, child, axis=0)
    row_parent = lax.dynamic_slice_in_dim(child_map, col_index % half_cols * row_items, row_items)
    col_parent = lax.dynamic_slice_in_dim(child_map, row_index * col_items, col_items)
    inv_k = (
        jnp.zeros((row_count,), jnp.int32)
        .at[row_parent // front_rows]
        .set(jnp.arange(row_items, dtype=jnp.int32))
    )
    inv_l = (
        jnp.full((col_count,), -1, jnp.int32)
        .at[col_parent // front_cols]
        .set(jnp.arange(col_items, dtype=jnp.int32))
    )
    fill_l = jnp.where(inv_l >= 0, inv_l, col_items)
    outgoing = (
        updates.reshape(row_items, BLK, col_items, BLK)
        .at[inv_k[:, None], :, fill_l[None, :], :]
        .get(mode="fill", fill_value=0.0)
        .reshape(devices_all, 1, BLK, BLK)
    )
    incoming = lax.all_to_all(
        outgoing, ("row", "col"), split_axis=0, concat_axis=0, tiled=True
    ).reshape(devices_all, BLK, BLK)
    my_rows = row_index * front_rows + jnp.arange(front_rows, dtype=jnp.int32)
    my_cols = col_index * front_cols + jnp.arange(front_cols, dtype=jnp.int32)
    lanes = jnp.arange(BLK, dtype=jnp.int32)
    front_local = None
    for child_id in range(2):
        inverse = (
            jnp.full((front_blocks,), -1, jnp.int32)
            .at[block_map[child_id]]
            .set(jnp.arange(block_map.shape[1], dtype=jnp.int32))
        )
        a = jnp.take(inverse, my_rows)
        b = jnp.take(inverse, my_cols)
        source = (jnp.maximum(b, 0) // col_items)[None, :] * col_count + (
            child_id * half_cols + jnp.maximum(a, 0) // row_items
        )[:, None]
        valid = (a >= 0)[:, None] & (b >= 0)[None, :]
        source = jnp.where(valid, source, devices_all)
        part = incoming.at[source[:, None, :], lanes[None, :, None], :].get(
            mode="fill", fill_value=0.0
        )
        front_local = part if front_local is None else front_local + part
    front_local = front_local.reshape(height, col_width)
    row_global = row_index * height + jnp.arange(height, dtype=jnp.int32)
    col_global = col_index * col_width + jnp.arange(col_width, dtype=jnp.int32)
    front_local = front_local + jnp.where(
        row_global[:, None] == col_global[None, :], own_diag[:, None], 0.0
    )
    piece_rows = height // col_count
    raw_panel = front_local[:, :PANEL]
    piece = jnp.where(col_index == 0, raw_panel[:piece_rows], 0.0)
    for k in range(1, col_count):
        pairs = [(r * col_count, r * col_count + k) for r in range(row_count)]
        piece = piece + lax.ppermute(
            raw_panel[k * piece_rows : (k + 1) * piece_rows], ("row", "col"), pairs
        )
    factor_piece = jnp.dot(
        piece, panel_inverse.T, precision=lax.Precision.HIGHEST, preferred_element_type=jnp.float32
    )
    factor_panel = lax.all_gather(factor_piece, "col", axis=0, tiled=True)
    ratio = col_count // row_count
    pairs = [
        (r * col_count + k, k % row_count * col_count + r * ratio + k // row_count)
        for r in range(row_count)
        for k in range(col_count)
    ]
    moved = lax.ppermute(factor_piece, ("row", "col"), pairs)
    stack = [moved]
    for q in range(1, row_count):
        shift = [(r, (r + q) % row_count) for r in range(row_count)]
        stack.append(lax.ppermute(moved, "row", shift))
    order = (row_index - jnp.arange(row_count, dtype=jnp.int32)) % row_count
    across = jnp.take(jnp.stack(stack), order, axis=0).reshape(col_width, PANEL)
    update_term = lax.dot_general(
        factor_panel,
        across,
        (((1,), (1,)), ((), ())),
        precision=lax.Precision.HIGHEST,
        preferred_element_type=jnp.float32,
    )
    trailing = front_local - update_term
    return (factor_panel, trailing)


def solution(mesh):
    return jax.shard_map(
        on_device,
        mesh=mesh,
        in_specs=(P("col", "row"), P(), P("row"), P()),
        out_specs=(P("row", None), P("row", "col")),
        check_vma=False,
    )
```

profile of v0, /device:TPU:0, one launch (start us, length us, event | category | flops | bytes accessed | tf_op | source)
XLA Modules:
  0.0 391.2 jit_solution(3016989263311851734)
XLA Ops:
  9.5 3.2 copy.17
  12.7 2.7 copy.12
  15.6 6.5 %gather_fusion = f32[128,128,128]{2,1,0:T(8,128)} fusion(f32[8,128,8,128]{3,1,2,0:T(8,128)} %copy.12, s32[128]{0:T(128)S(1)} %reshape.345), kind=kCustom, calls=%fused_computation.4 | custom fusion | bytes 16778240 | tf_op jit(solution)/shard_map/gather | solution.py:46
  22.1 7.2 %fusion = f32[128,1,128,128]{3,2,1,0:T(8,128)} fusion(f32[128,128,128]{2,1,0:T(8,128)} %gather_fusion, pred[128]{0:T(512)(128)(4,1)S(1)} %broadcast_in_dim.136), kind=kLoop, calls=%fused_computation.13 | loop fusion | flops 2097152 | bytes 16777344 | tf_op jit(solution)/shard_map/select_n | solution.py:46
  29.3 11.7 %all-to-all-start = ((f32[128,1,128,128]{3,2,1,0:T(8,128)}), f32[128,1,128,128]{3,2,1,0:T(8,128)}, u32[]{:S(2)}, u32[]{:S(2)}) async-start(f32[128,1,128,128]{3,2,1,0:T(8,128)} %fusion), calls=%async_computation | async-start | bytes 16777216 | tf_op jit(solution)/shard_map/all_to_all | solution.py:49
  48.4 90.6 %all-to-all-done = f32[128,1,128,128]{3,2,1,0:T(8,128)} async-done(((f32[128,1,128,128]{3,2,1,0:T(8,128)}), f32[128,1,128,128]{3,2,1,0:T(8,128)}, u32[]{:S(2)}, u32[]{:S(2)}) %all-to-all-start) | async-done | bytes 8388640 | tf_op jit(solution)/shard_map/all_to_all | solution.py:49
  139.0 61.8 %gather_fusion.1 = f32[6400,128]{1,0:T(8,128)} fusion(f32[128,128,128]{2,1,0:T(8,128)} %bitcast.8, s32[6400]{0:T(1024)S(1)} %reshape.351), kind=kCustom, calls=%fused_computation.5 | custom fusion | bytes 6604800 | tf_op jit(solution)/shard_map/gather | solution.py:69
  200.8 4.9 %reshape.354 = f32[10,128,5,128]{3,2,1,0:T(8,128)} reshape(f32[6400,128]{1,0:T(8,128)} %gather_fusion.1) | data formatting | bytes 6553600 | tf_op jit(solution)/shard_map/gather | solution.py:69
  205.7 61.7 %gather_fusion.2 = f32[6400,128]{1,0:T(8,128)} fusion(f32[128,128,128]{2,1,0:T(8,128)} %bitcast.8, s32[6400]{0:T(1024)S(1)} %reshape.357), kind=kCustom, calls=%fused_computation.6 | custom fusion | bytes 6604800 | tf_op jit(solution)/shard_map/gather | solution.py:69
  267.4 4.9 %reshape.360 = f32[10,128,5,128]{3,2,1,0:T(8,128)} reshape(f32[6400,128]{1,0:T(8,128)} %gather_fusion.2) | data formatting | bytes 6553600 | tf_op jit(solution)/shard_map/gather | solution.py:69
  272.3 5.5 %select_add_fusion = f32[10,128,5,128]{3,2,1,0:T(8,128)S(1)} fusion(f32[10,128,5,128]{3,2,1,0:T(8,128)} %reshape.360, f32[10,128,5,128]{3,2,1,0:T(8,128)} %reshape.354, pred[10,128,5]{2,1,0:T(8,128)(4,1)S(1)} %copy.15, pred[10,128,5]{2,1,0:T(8,128)(4,1)S(1)} %copy.11), kind=kLoop, calls=%fused_computation.14 | loop fusion | flops 2457600 | bytes 9843200 | tf_op jit(solution)/shard_map/add | solution.py:72
  280.5 2.7 collective-permute-start
  283.3 3.5 collective-permute-start.1
  286.8 3.3 collective-permute-start.10
  300.8 2.2 collective-permute-done.13
  303.0 1.9 collective-permute-start.5
  305.3 2.1 collective-permute-start.6
  307.4 2.0 collective-permute-start.7
  309.4 1.9 collective-permute-start.8
  311.3 2.0 collective-permute-start.9
  313.3 3.3 collective-permute-done.7
  316.6 3.5 collective-permute-done.8
  320.1 2.3 collective-permute-done.9
  322.4 3.1 fusion.16
  327.3 6.0 %collective-permute-start.16 = (f32[80,512]{1,0:T(8,128)S(1)}, f32[80,512]{1,0:T(8,128)S(1)}, u32[]{:S(2)}, u32[]{:S(2)}) collective-permute-start(f32[80,512]{1,0:T(8,128)S(1)} %collective-permute-done.15), channel_id=1, source_target_pairs={{0,16},{16,32},{32,48},{48,64},{64,80},{80,96},{96,112},{112,0},{1... | collective-permute-start | bytes 491528 | tf_op jit(solution)/shard_map/ppermute | solution.py:101
  333.4 7.3 %collective-permute-start.17 = (f32[80,512]{1,0:T(8,128)S(1)}, f32[80,512]{1,0:T(8,128)S(1)}, u32[]{:S(2)}, u32[]{:S(2)}) collective-permute-start(f32[80,512]{1,0:T(8,128)S(1)} %collective-permute-done.15), channel_id=1, source_target_pairs={{0,32},{16,48},{32,64},{48,80},{64,96},{80,112},{96,0},{112,16},{1... | collective-permute-start | bytes 491528 | tf_op jit(solution)/shard_map/ppermute | solution.py:101
  341.1 3.7 collective-permute-start.19
  344.8 1.9 collective-permute-start.21
  346.7 2.8 collective-permute-start.22
  349.5 3.1 collective-permute-done.18
  359.6 13.5 %all-gather.2.cloned.1.call-done = f32[1280,512]{1,0:T(8,128)} async-done(((f32[80,512]{1,0:T(8,128)}), f32[1280,512]{1,0:T(8,128)}) %all-gather.2.cloned.1.call-update) | async-done | bytes 2621456 | tf_op jit(solution)/shard_map/all_gather | solution.py:90
  373.1 9.8 %convolution_subtract_fusion = f32[1280,640]{1,0:T(8,128)} fusion(f32[1280,640]{1,0:T(8,128)} %copy-done.1, f32[1280,512]{1,0:T(8,128)} %all-gather.2.cloned.1.call-done, f32[640,512]{1,0:T(8,128)S(1)} %bitcast_select_fusion.1), kind=kOutput, calls=%fused_computation.15 | convolution fusion | flops 5033984000 | bytes 10485760 | tf_op jit(solution)/shard_map/dot_general | solution.py:104
  (105 shorter events, 34.0 us)
Async XLA Ops:
  7.2 315.2 %copy-start = (f32[512,512]{1,0:T(8,128)S(1)}, f32[512,512]{1,0:T(8,128)}, u32[]{:S(2)}) copy-start(f32[512,512]{1,0:T(8,128)} %param.11) | copy-start | bytes 3145732
  29.3 11.8 %copy-start.4 = (s32[2,64]{1,0:T(2,128)S(1)}, s32[2,64]{1,0:T(2,128)}, u32[]{:S(2)}) copy-start(s32[2,64]{1,0:T(2,128)} %param.9) | copy-start | bytes 1540
  29.3 109.8 %all-to-all-start = ((f32[128,1,128,128]{3,2,1,0:T(8,128)}), f32[128,1,128,128]{3,2,1,0:T(8,128)}, u32[]{:S(2)}, u32[]{:S(2)}) async-start(f32[128,1,128,128]{3,2,1,0:T(8,128)} %fusion), calls=%async_computation | async-start | bytes 16777216 | tf_op jit(solution)/shard_map/all_to_all | solution.py:49
  41.0 332.1 %all-gather.2.cloned.1.call-start = ((), (), s32[]{:S(2)}) async-start(), calls=%async_computation.1 | async-start | bytes 2785280 | tf_op jit(solution)/shard_map/all_gather | solution.py:90
  272.3 5.6 %copy-start.3 = (f32[1280]{0:T(1024)S(1)}, f32[1280]{0:T(1024)}, u32[]{:S(2)}) copy-start(f32[1280]{0:T(1024)} %param.10) | copy-start | bytes 15364
  278.6 1.7 copy-start.1
  280.5 12.2 %collective-permute-start = (f32[80,512]{1,0:T(8,128)S(1)}, f32[80,512]{1,0:T(8,128)S(1)}, u32[]{:S(2)}, u32[]{:S(2)}) collective-permute-start(f32[80,512]{1,0:T(8,128)S(1)} %get-tuple-element.19), channel_id=1, source_target_pairs={{0,1},{16,17},{32,33},{48,49},{64,65},{80,81},{96,97},{112,113}} | collective-permute-start | bytes 491528 | tf_op jit(solution)/shard_map/ppermute | solution.py:84
  283.3 10.8 %collective-permute-start.1 = (f32[80,512]{1,0:T(8,128)S(1)}, f32[80,512]{1,0:T(8,128)S(1)}, u32[]{:S(2)}, u32[]{:S(2)}) collective-permute-start(f32[80,512]{1,0:T(8,128)S(1)} %get-tuple-element.33), channel_id=1, source_target_pairs={{0,2},{16,18},{32,34},{48,50},{64,66},{80,82},{96,98},{112,114}} | collective-permute-start | bytes 491528 | tf_op jit(solution)/shard_map/ppermute | solution.py:84
  286.8 8.6 %collective-permute-start.10 = (f32[80,512]{1,0:T(8,128)S(1)}, f32[80,512]{1,0:T(8,128)S(1)}, u32[]{:S(2)}, u32[]{:S(2)}) collective-permute-start(f32[80,512]{1,0:T(8,128)S(1)} %get-tuple-element.24), channel_id=1, source_target_pairs={{0,11},{16,27},{32,43},{48,59},{64,75},{80,91},{96,107},{112,123}} | collective-permute-start | bytes 491528 | tf_op jit(solution)/shard_map/ppermute | solution.py:84
  290.1 6.6 %collective-permute-start.11 = (f32[80,512]{1,0:T(8,128)S(1)}, f32[80,512]{1,0:T(8,128)S(1)}, u32[]{:S(2)}, u32[]{:S(2)}) collective-permute-start(f32[80,512]{1,0:T(8,128)S(1)} %get-tuple-element.23), channel_id=1, source_target_pairs={{0,12},{16,28},{32,44},{48,60},{64,76},{80,92},{96,108},{112,124}} | collective-permute-start | bytes 491528 | tf_op jit(solution)/shard_map/ppermute | solution.py:84
  291.4 8.1 %collective-permute-start.12 = (f32[80,512]{1,0:T(8,128)S(1)}, f32[80,512]{1,0:T(8,128)S(1)}, u32[]{:S(2)}, u32[]{:S(2)}) collective-permute-start(f32[80,512]{1,0:T(8,128)S(1)} %get-tuple-element.22), channel_id=1, source_target_pairs={{0,13},{16,29},{32,45},{48,61},{64,77},{80,93},{96,109},{112,125}} | collective-permute-start | bytes 491528 | tf_op jit(solution)/shard_map/ppermute | solution.py:84
  292.7 10.3 %collective-permute-start.13 = (f32[80,512]{1,0:T(8,128)S(1)}, f32[80,512]{1,0:T(8,128)S(1)}, u32[]{:S(2)}, u32[]{:S(2)}) collective-permute-start(f32[80,512]{1,0:T(8,128)S(1)} %get-tuple-element.21), channel_id=1, source_target_pairs={{0,14},{16,30},{32,46},{48,62},{64,78},{80,94},{96,110},{112,126}} | collective-permute-start | bytes 491528 | tf_op jit(solution)/shard_map/ppermute | solution.py:84
  294.0 11.2 %collective-permute-start.14 = (f32[80,512]{1,0:T(8,128)S(1)}, f32[80,512]{1,0:T(8,128)S(1)}, u32[]{:S(2)}, u32[]{:S(2)}) collective-permute-start(f32[80,512]{1,0:T(8,128)S(1)} %get-tuple-element.20), channel_id=1, source_target_pairs={{0,15},{16,31},{32,47},{48,63},{64,79},{80,95},{96,111},{112,127}} | collective-permute-start | bytes 491528 | tf_op jit(solution)/shard_map/ppermute | solution.py:84
  295.4 12.1 %collective-permute-start.2 = (f32[80,512]{1,0:T(8,128)S(1)}, f32[80,512]{1,0:T(8,128)S(1)}, u32[]{:S(2)}, u32[]{:S(2)}) collective-permute-start(f32[80,512]{1,0:T(8,128)S(1)} %get-tuple-element.32), channel_id=1, source_target_pairs={{0,3},{16,19},{32,35},{48,51},{64,67},{80,83},{96,99},{112,115}} | collective-permute-start | bytes 491528 | tf_op jit(solution)/shard_map/ppermute | solution.py:84
  296.7 12.7 %collective-permute-start.3 = (f32[80,512]{1,0:T(8,128)S(1)}, f32[80,512]{1,0:T(8,128)S(1)}, u32[]{:S(2)}, u32[]{:S(2)}) collective-permute-start(f32[80,512]{1,0:T(8,128)S(1)} %get-tuple-element.31), channel_id=1, source_target_pairs={{0,4},{16,20},{32,36},{48,52},{64,68},{80,84},{96,100},{112,116}} | collective-permute-start | bytes 491528 | tf_op jit(solution)/shard_map/ppermute | solution.py:84
  299.5 11.8 %collective-permute-start.4 = (f32[80,512]{1,0:T(8,128)S(1)}, f32[80,512]{1,0:T(8,128)S(1)}, u32[]{:S(2)}, u32[]{:S(2)}) collective-permute-start(f32[80,512]{1,0:T(8,128)S(1)} %get-tuple-element.30), channel_id=1, source_target_pairs={{0,5},{16,21},{32,37},{48,53},{64,69},{80,85},{96,101},{112,117}} | collective-permute-start | bytes 491528 | tf_op jit(solution)/shard_map/ppermute | solution.py:84
  303.0 10.3 %collective-permute-start.5 = (f32[80,512]{1,0:T(8,128)S(1)}, f32[80,512]{1,0:T(8,128)}, u32[]{:S(2)}, u32[]{:S(2)}) collective-permute-start(f32[80,512]{1,0:T(8,128)S(1)} %get-tuple-element.29), channel_id=1, source_target_pairs={{0,6},{16,22},{32,38},{48,54},{64,70},{80,86},{96,102},{112,118}} | collective-permute-start | bytes 491528 | tf_op jit(solution)/shard_map/ppermute | solution.py:84
  305.3 8.0 %collective-permute-start.6 = (f32[80,512]{1,0:T(8,128)S(1)}, f32[80,512]{1,0:T(8,128)}, u32[]{:S(2)}, u32[]{:S(2)}) collective-permute-start(f32[80,512]{1,0:T(8,128)S(1)} %get-tuple-element.28), channel_id=1, source_target_pairs={{0,7},{16,23},{32,39},{48,55},{64,71},{80,87},{96,103},{112,119}} | collective-permute-start | bytes 491528 | tf_op jit(solution)/shard_map/ppermute | solution.py:84
  307.4 9.2 %collective-permute-start.7 = (f32[80,512]{1,0:T(8,128)S(1)}, f32[80,512]{1,0:T(8,128)}, u32[]{:S(2)}, u32[]{:S(2)}) collective-permute-start(f32[80,512]{1,0:T(8,128)S(1)} %get-tuple-element.27), channel_id=1, source_target_pairs={{0,8},{16,24},{32,40},{48,56},{64,72},{80,88},{96,104},{112,120}} | collective-permute-start | bytes 491528 | tf_op jit(solution)/shard_map/ppermute | solution.py:84
  309.4 10.7 %collective-permute-start.8 = (f32[80,512]{1,0:T(8,128)S(1)}, f32[80,512]{1,0:T(8,128)}, u32[]{:S(2)}, u32[]{:S(2)}) collective-permute-start(f32[80,512]{1,0:T(8,128)S(1)} %get-tuple-element.26), channel_id=1, source_target_pairs={{0,9},{16,25},{32,41},{48,57},{64,73},{80,89},{96,105},{112,121}} | collective-permute-start | bytes 491528 | tf_op jit(solution)/shard_map/ppermute | solution.py:84
  311.3 11.1 %collective-permute-start.9 = (f32[80,512]{1,0:T(8,128)S(1)}, f32[80,512]{1,0:T(8,128)}, u32[]{:S(2)}, u32[]{:S(2)}) collective-permute-start(f32[80,512]{1,0:T(8,128)S(1)} %get-tuple-element.25), channel_id=1, source_target_pairs={{0,10},{16,26},{32,42},{48,58},{64,74},{80,90},{96,106},{112,122}} | collective-permute-start | bytes 491528 | tf_op jit(solution)/shard_map/ppermute | solution.py:84
  325.6 1.8 collective-permute-start.15
  327.3 17.5 %collective-permute-start.16 = (f32[80,512]{1,0:T(8,128)S(1)}, f32[80,512]{1,0:T(8,128)S(1)}, u32[]{:S(2)}, u32[]{:S(2)}) collective-permute-start(f32[80,512]{1,0:T(8,128)S(1)} %collective-permute-done.15), channel_id=1, source_target_pairs={{0,16},{16,32},{32,48},{48,64},{64,80},{80,96},{96,112},{112,0},{1... | collective-permute-start | bytes 491528 | tf_op jit(solution)/shard_map/ppermute | solution.py:101
  333.4 13.3 %collective-permute-start.17 = (f32[80,512]{1,0:T(8,128)S(1)}, f32[80,512]{1,0:T(8,128)S(1)}, u32[]{:S(2)}, u32[]{:S(2)}) collective-permute-start(f32[80,512]{1,0:T(8,128)S(1)} %collective-permute-done.15), channel_id=1, source_target_pairs={{0,32},{16,48},{32,64},{48,80},{64,96},{80,112},{96,0},{112,16},{1... | collective-permute-start | bytes 491528 | tf_op jit(solution)/shard_map/ppermute | solution.py:101
  340.6 11.9 %collective-permute-start.18 = (f32[80,512]{1,0:T(8,128)S(1)}, f32[80,512]{1,0:T(8,128)S(1)}, u32[]{:S(2)}, u32[]{:S(2)}) collective-permute-start(f32[80,512]{1,0:T(8,128)S(1)} %collective-permute-done.15), channel_id=1, source_target_pairs={{0,48},{16,64},{32,80},{48,96},{64,112},{80,0},{96,16},{112,32},{1... | collective-permute-start | bytes 491528 | tf_op jit(solution)/shard_map/ppermute | solution.py:101
  341.1 12.7 %collective-permute-start.19 = (f32[80,512]{1,0:T(8,128)S(1)}, f32[80,512]{1,0:T(8,128)S(1)}, u32[]{:S(2)}, u32[]{:S(2)}) collective-permute-start(f32[80,512]{1,0:T(8,128)S(1)} %collective-permute-done.15), channel_id=1, source_target_pairs={{0,64},{16,80},{32,96},{48,112},{64,0},{80,16},{96,32},{112,48},{1... | collective-permute-start | bytes 491528 | tf_op jit(solution)/shard_map/ppermute | solution.py:101
  344.8 10.4 %collective-permute-start.20 = (f32[80,512]{1,0:T(8,128)S(1)}, f32[80,512]{1,0:T(8,128)S(1)}, u32[]{:S(2)}, u32[]{:S(2)}) collective-permute-start(f32[80,512]{1,0:T(8,128)S(1)} %collective-permute-done.15), channel_id=1, source_target_pairs={{0,80},{16,96},{32,112},{48,0},{64,16},{80,32},{96,48},{112,64},{1... | collective-permute-start | bytes 491528 | tf_op jit(solution)/shard_map/ppermute | solution.py:101
  344.8 10.9 %collective-permute-start.21 = (f32[80,512]{1,0:T(8,128)S(1)}, f32[80,512]{1,0:T(8,128)S(1)}, u32[]{:S(2)}, u32[]{:S(2)}) collective-permute-start(f32[80,512]{1,0:T(8,128)S(1)} %collective-permute-done.15), channel_id=1, source_target_pairs={{0,96},{16,112},{32,0},{48,16},{64,32},{80,48},{96,64},{112,80},{1... | collective-permute-start | bytes 491528 | tf_op jit(solution)/shard_map/ppermute | solution.py:101
  346.7 9.7 %collective-permute-start.22 = (f32[80,512]{1,0:T(8,128)S(1)}, f32[80,512]{1,0:T(8,128)S(1)}, u32[]{:S(2)}, u32[]{:S(2)}) collective-permute-start(f32[80,512]{1,0:T(8,128)S(1)} %collective-permute-done.15), channel_id=1, source_target_pairs={{0,112},{16,0},{32,16},{48,32},{64,48},{80,64},{96,80},{112,96},{1... | collective-permute-start | bytes 491528 | tf_op jit(solution)/shard_map/ppermute | solution.py:101
  373.1 9.8 %copy-start.2 = (f32[1280,512]{1,0:T(8,128)S(1)}, f32[1280,512]{1,0:T(8,128)}, u32[]{:S(2)}) copy-start(f32[1280,512]{1,0:T(8,128)} %all-gather.2.cloned.1.call-done) | copy-start | bytes 7864324
Sparse Core Ops, SparseCore 0:
  325.7 47.3 all-gather.1
where the time goes:
time: 393 us; the launch traced here: 391 us
  local copies, waits for them, and re-layouts  159 us (40%)
  waiting for transfers between devices  124 us (32%)
  starting transfers between devices  63.9 us (16%)
  other arithmetic  16.6 us (4%)
  between operations  14.6 us (4%)
  matrix products  12.9 us (3%)
    gather x4, local copies, waits for them, and re-layouts, on_device(): incoming.at[source[:, None, :], lanes[None, :, None], :]  133 us
    all_to_all x1, waiting for transfers between devices, on_device(): lax.all_to_all(outgoing, ('row', 'col'), split_axis=0, concat_axis=0, til...  90.6 us
    ppermute x15, starting transfers between devices, on_device(): lax.ppermute(raw_panel[k * piece_rows:(k + 1) * piece_rows], ('row', 'col...  28.6 us
    ppermute x7, starting transfers between devices, on_device(): stack.append(lax.ppermute(moved, 'row', shift))  22 us
    all_gather x1, waiting for transfers between devices, on_device(): factor_panel = lax.all_gather(factor_piece, 'col', axis=0, tiled=True)  13.5 us
    ppermute x15, waiting for transfers between devices, on_device(): lax.ppermute(raw_panel[k * piece_rows:(k + 1) * piece_rows], ('row', 'col...  13.2 us
    all_to_all x1, starting transfers between devices, on_device(): lax.all_to_all(outgoing, ('row', 'col'), split_axis=0, concat_axis=0, til...  11.7 us
    dot_general x1, matrix products, on_device(): lax.dot_general(factor_panel, across, (((1,), (1,)), ((), ())), precision...  9.78 us
  transfers between devices with their start and end apart: 25, of which 13 were waited for; matrix products, arithmetic and copies ran while one was open for 3% of the time, Pallas kernels for 0%

commit v1 on v0

--- a/solution.py
+++ b/solution.py
@@ -7,6 +7,12 @@
 M = 8192
 BLK = 128
 PANEL = 512
+
+
+def _direct_samples(obj, row_dim):
+    last = list(obj.shape[1:])
+    last[row_dim] *= obj.shape[0]
+    return jnp.moveaxis(obj, 0, row_dim).reshape(last)
 
 
 def on_device(updates, block_map, own_diag, panel_inverse):
@@ -87,7 +93,23 @@
     factor_piece = jnp.dot(
         piece, panel_inverse.T, precision=lax.Precision.HIGHEST, preferred_element_type=jnp.float32
     )
-    factor_panel = lax.all_gather(factor_piece, "col", axis=0, tiled=True)
+    axis_n = lax.axis_size("col")
+    parts_seen = []
+    for dev in range(axis_n):
+        parts_seen.append((dev, (dev + 1) % axis_n))
+    stack_in = []
+    for h, rr in parts_seen:
+        stack_in.append((rr, h))
+    formed, f_now = ([], [])
+    for idx in range(axis_n - 1):
+        if idx % 2 == 0:
+            formed.append(lax.ppermute(formed[-1] if formed else factor_piece, "col", parts_seen))
+        else:
+            f_now.append(lax.ppermute(f_now[-1] if f_now else factor_piece, "col", stack_in))
+    everything = jnp.stack([*formed[::-1], factor_piece, *f_now])
+    a_now = lax.axis_index("col") - len(formed)
+    everything = everything[(jnp.arange(axis_n) - a_now) % axis_n]
+    factor_panel = _direct_samples(everything, 0)
     ratio = col_count // row_count
     pairs = [
         (r * col_count + k, k % row_count * col_count + r * ratio + k // row_count)

time: 393 us -> 435 us (1.11)
  starting transfers between devices: 63.9 us -> 93.8 us
  local copies, waits for them, and re-layouts: 159 us -> 176 us
  between operations: 14.6 us -> 1.33 us
  waiting for transfers between devices: 124 us -> 134 us
    ppermute x0 -> x15, starting transfers between devices: none -> 33.6 us  [the longest x7 31.7 us: on_device(): lax.ppermute(f_now[-1] if f_now else factor_piece, 'col', stack_in)]
    ppermute x0 -> x15, waiting for transfers between devices: none -> 26.4 us  [the longest x8 26 us: on_device(): lax.ppermute(formed[-1] if formed else factor_piece, 'col', parts_seen)]
    all_gather x1 -> x0, waiting for transfers between devices: 13.5 us -> none  [on_device(): factor_panel = lax.all_gather(factor_piece, 'col', axis=0, tiled=True)]
    unnamed x19 -> x39, local copies, waits for them, and re-layouts: 6.5 us -> 18.8 us
  transfers between devices with their start and end apart: 25 -> 39, of which waited for: 13 -> 16; matrix products, arithmetic and copies ran while one was open for 3% -> 6% of each run, Pallas kernels for 0% -> 0%
where the time goes in v1:
time: 435 us; the launch traced here: 434 us
  local copies, waits for them, and re-layouts  176 us (40%)
  waiting for transfers between devices  134 us (31%)
  starting transfers between devices  93.8 us (22%)
  other arithmetic  16.8 us (4%)
  matrix products  12.1 us (3%)
    gather x4, local copies, waits for them, and re-layouts, on_device(): incoming.at[source[:, None, :], lanes[None, :, None], :]  133 us
    all_to_all x1, waiting for transfers between devices, on_device(): lax.all_to_all(outgoing, ('row', 'col'), split_axis=0, concat_axis=0, til...  90.7 us
    ppermute x7, starting transfers between devices, on_device(): lax.ppermute(f_now[-1] if f_now else factor_piece, 'col', stack_in)  31.7 us
    ppermute x15, starting transfers between devices, on_device(): lax.ppermute(raw_panel[k * piece_rows:(k + 1) * piece_rows], ('row', 'col...  28.5 us
    ppermute x8, waiting for transfers between devices, on_device(): lax.ppermute(formed[-1] if formed else factor_piece, 'col', parts_seen)  26 us
    ppermute x7, starting transfers between devices, on_device(): stack.append(lax.ppermute(moved, 'row', shift))  19.3 us
    unnamed x39, local copies, waits for them, and re-layouts  18.8 us
    ppermute x15, waiting for transfers between devices, on_device(): lax.ppermute(raw_panel[k * piece_rows:(k + 1) * piece_rows], ('row', 'col...  13.1 us
  transfers between devices with their start and end apart: 39, of which 16 were waited for; matrix products, arithmetic and copies ran while one was open for 6% of the time, Pallas kernels for 0%

profile of v1, /device:TPU:0, one launch (start us, length us, event | category | flops | bytes accessed | tf_op | source)
XLA Modules:
  0.0 433.8 jit_solution(6083016939844018700)
XLA Ops:
  3.0 3.2 copy.17
  6.2 2.7 copy.12
  9.1 6.5 %gather_fusion = f32[128,128,128]{2,1,0:T(8,128)} fusion(f32[8,128,8,128]{3,1,2,0:T(8,128)} %copy.12, s32[128]{0:T(128)S(1)} %reshape.428), kind=kCustom, calls=%fused_computation.4 | custom fusion | bytes 16778240 | tf_op jit(solution)/shard_map/gather | solution.py:52
  15.6 7.2 %fusion = f32[128,1,128,128]{3,2,1,0:T(8,128)} fusion(f32[128,128,128]{2,1,0:T(8,128)} %gather_fusion, pred[128]{0:T(512)(128)(4,1)S(1)} %broadcast_in_dim.133), kind=kLoop, calls=%fused_computation.14 | loop fusion | flops 2097152 | bytes 16777344 | tf_op jit(solution)/shard_map/select_n | solution.py:52
  22.8 11.7 %all-to-all-start = ((f32[128,1,128,128]{3,2,1,0:T(8,128)}), f32[128,1,128,128]{3,2,1,0:T(8,128)}, u32[]{:S(2)}, u32[]{:S(2)}) async-start(f32[128,1,128,128]{3,2,1,0:T(8,128)} %fusion), calls=%async_computation | async-start | bytes 16777216 | tf_op jit(solution)/shard_map/all_to_all | solution.py:55
  41.9 90.7 %all-to-all-done = f32[128,1,128,128]{3,2,1,0:T(8,128)} async-done(((f32[128,1,128,128]{3,2,1,0:T(8,128)}), f32[128,1,128,128]{3,2,1,0:T(8,128)}, u32[]{:S(2)}, u32[]{:S(2)}) %all-to-all-start) | async-done | bytes 8388640 | tf_op jit(solution)/shard_map/all_to_all | solution.py:55
  132.6 61.7 %gather_fusion.1 = f32[6400,128]{1,0:T(8,128)} fusion(f32[128,128,128]{2,1,0:T(8,128)} %bitcast.8, s32[6400]{0:T(1024)S(1)} %reshape.434), kind=kCustom, calls=%fused_computation.5 | custom fusion | bytes 6604800 | tf_op jit(solution)/shard_map/gather | solution.py:75
  194.2 4.8 %reshape.437 = f32[10,128,5,128]{3,2,1,0:T(8,128)} reshape(f32[6400,128]{1,0:T(8,128)} %gather_fusion.1) | data formatting | bytes 6553600 | tf_op jit(solution)/shard_map/gather | solution.py:75
  199.1 61.7 %gather_fusion.2 = f32[6400,128]{1,0:T(8,128)} fusion(f32[128,128,128]{2,1,0:T(8,128)} %bitcast.8, s32[6400]{0:T(1024)S(1)} %reshape.440), kind=kCustom, calls=%fused_computation.6 | custom fusion | bytes 6604800 | tf_op jit(solution)/shard_map/gather | solution.py:75
  260.8 4.9 %reshape.443 = f32[10,128,5,128]{3,2,1,0:T(8,128)} reshape(f32[6400,128]{1,0:T(8,128)} %gather_fusion.2) | data formatting | bytes 6553600 | tf_op jit(solution)/shard_map/gather | solution.py:75
  265.7 5.5 %select_add_fusion = f32[10,128,5,128]{3,2,1,0:T(8,128)S(1)} fusion(f32[10,128,5,128]{3,2,1,0:T(8,128)} %reshape.443, f32[10,128,5,128]{3,2,1,0:T(8,128)} %reshape.437, pred[10,128,5]{2,1,0:T(8,128)(4,1)S(1)} %copy.15, pred[10,128,5]{2,1,0:T(8,128)(4,1)S(1)} %copy.11), kind=kLoop, calls=%fused_computation.15 | loop fusion | flops 2457600 | bytes 9843200 | tf_op jit(solution)/shard_map/add | solution.py:78
  276.6 3.6 collective-permute-start.1
  280.2 3.2 collective-permute-start.10
  306.6 3.3 collective-permute-done.7
  309.9 3.5 collective-permute-done.8
  320.6 3.6 collective-permute-start.23
  324.2 3.7 collective-permute-start.31
  327.9 8.3 %collective-permute-start.32 = (f32[80,512]{1,0:T(8,128)S(1)}, f32[80,512]{1,0:T(8,128)S(1)}, u32[]{:S(2)}, u32[]{:S(2)}) collective-permute-start(f32[80,512]{1,0:T(8,128)S(1)} %collective-permute-done.30), channel_id=1, source_target_pairs={{0,32},{16,48},{32,64},{48,80},{64,96},{80,112},{96,0},{112,16},{1... | collective-permute-start | bytes 491528 | tf_op jit(solution)/shard_map/ppermute | solution.py:123
  336.3 5.7 %collective-permute-start.34 = (f32[80,512]{1,0:T(8,128)S(1)}, f32[80,512]{1,0:T(8,128)S(1)}, u32[]{:S(2)}, u32[]{:S(2)}) collective-permute-start(f32[80,512]{1,0:T(8,128)S(1)} %collective-permute-done.30), channel_id=1, source_target_pairs={{0,64},{16,80},{32,96},{48,112},{64,0},{80,16},{96,32},{112,48},{1... | collective-permute-start | bytes 491528 | tf_op jit(solution)/shard_map/ppermute | solution.py:123
  343.1 4.0 collective-permute-done.33
  348.5 4.0 collective-permute-done.16
  353.5 4.8 %collective-permute-start.25 = (f32[80,512]{1,0:T(8,128)S(1)}, f32[80,512]{1,0:T(8,128)S(1)}, u32[]{:S(2)}, u32[]{:S(2)}) collective-permute-start(f32[80,512]{1,0:T(8,128)S(1)} %collective-permute-done.24), channel_id=1, source_target_pairs={{1,0},{2,1},{3,2},{4,3},{5,4},{6,5},{7,6},{8,7},{9,8},{10,9},{11,1... | collective-permute-start | bytes 491528 | tf_op jit(solution)/shard_map/ppermute | solution.py:108
  358.4 3.6 collective-permute-done.17
  362.0 8.6 %collective-permute-done.18 = f32[80,512]{1,0:T(8,128)S(1)} collective-permute-done((f32[80,512]{1,0:T(8,128)S(1)}, f32[80,512]{1,0:T(8,128)S(1)}, u32[]{:S(2)}, u32[]{:S(2)}) %collective-permute-start.18) | collective-permute-done | bytes 163872 | tf_op jit(solution)/shard_map/ppermute | solution.py:106
  370.6 5.4 %collective-permute-start.26 = (f32[80,512]{1,0:T(8,128)S(1)}, f32[80,512]{1,0:T(8,128)}, u32[]{:S(2)}, u32[]{:S(2)}) collective-permute-start(f32[80,512]{1,0:T(8,128)S(1)} %collective-permute-done.25), channel_id=1, source_target_pairs={{1,0},{2,1},{3,2},{4,3},{5,4},{6,5},{7,6},{8,7},{9,8},{10,9},{11,1... | collective-permute-start | bytes 491528 | tf_op jit(solution)/shard_map/ppermute | solution.py:108
  376.0 3.2 collective-permute-done.19
  379.3 5.5 %collective-permute-start.27 = (f32[80,512]{1,0:T(8,128)}, f32[80,512]{1,0:T(8,128)}, u32[]{:S(2)}, u32[]{:S(2)}) collective-permute-start(f32[80,512]{1,0:T(8,128)} %collective-permute-done.26), channel_id=1, source_target_pairs={{1,0},{2,1},{3,2},{4,3},{5,4},{6,5},{7,6},{8,7},{9,8},{10,9},{11,1... | collective-permute-start | bytes 491528 | tf_op jit(solution)/shard_map/ppermute | solution.py:108
  384.8 3.2 collective-permute-done.20
  389.7 5.4 %collective-permute-start.28 = (f32[80,512]{1,0:T(8,128)}, f32[80,512]{1,0:T(8,128)S(1)}, u32[]{:S(2)}, u32[]{:S(2)}) collective-permute-start(f32[80,512]{1,0:T(8,128)} %collective-permute-done.27), channel_id=1, source_target_pairs={{1,0},{2,1},{3,2},{4,3},{5,4},{6,5},{7,6},{8,7},{9,8},{10,9},{11,1... | collective-permute-start | bytes 491528 | tf_op jit(solution)/shard_map/ppermute | solution.py:108
  398.5 5.6 %collective-permute-start.29 = (f32[80,512]{1,0:T(8,128)S(1)}, f32[80,512]{1,0:T(8,128)S(1)}, u32[]{:S(2)}, u32[]{:S(2)}) collective-permute-start(f32[80,512]{1,0:T(8,128)S(1)} %collective-permute-done.28), channel_id=1, source_target_pairs={{1,0},{2,1},{3,2},{4,3},{5,4},{6,5},{7,6},{8,7},{9,8},{10,9},{11,1... | collective-permute-start | bytes 491528 | tf_op jit(solution)/shard_map/ppermute | solution.py:108
  420.2 3.9 gather_fusion.3
  424.2 9.6 %convolution_subtract_fusion = f32[1280,640]{1,0:T(8,128)} fusion(f32[1280,640]{1,0:T(8,128)} %copy-done.1, f32[1280,512]{1,0:T(8,128)} %bitcast.107, f32[640,512]{1,0:T(8,128)S(1)} %bitcast.109), kind=kOutput, calls=%fused_computation.16 | convolution fusion | flops 5033984000 | bytes 10485760 | tf_op jit(solution)/shard_map/dot_general | solution.py:126
  (154 shorter events, 69.8 us)
Async XLA Ops:
  22.8 109.8 %all-to-all-start = ((f32[128,1,128,128]{3,2,1,0:T(8,128)}), f32[128,1,128,128]{3,2,1,0:T(8,128)}, u32[]{:S(2)}, u32[]{:S(2)}) async-start(f32[128,1,128,128]{3,2,1,0:T(8,128)} %fusion), calls=%async_computation | async-start | bytes 16777216 | tf_op jit(solution)/shard_map/all_to_all | solution.py:55
  273.9 12.1 %collective-permute-start = (f32[80,512]{1,0:T(8,128)S(1)}, f32[80,512]{1,0:T(8,128)S(1)}, u32[]{:S(2)}, u32[]{:S(2)}) collective-permute-start(f32[80,512]{1,0:T(8,128)S(1)} %get-tuple-element.19), channel_id=1, source_target_pairs={{0,1},{16,17},{32,33},{48,49},{64,65},{80,81},{96,97},{112,113}} | collective-permute-start | bytes 491528 | tf_op jit(solution)/shard_map/ppermute | solution.py:90
  276.6 10.8 %collective-permute-start.1 = (f32[80,512]{1,0:T(8,128)S(1)}, f32[80,512]{1,0:T(8,128)S(1)}, u32[]{:S(2)}, u32[]{:S(2)}) collective-permute-start(f32[80,512]{1,0:T(8,128)S(1)} %get-tuple-element.33), channel_id=1, source_target_pairs={{0,2},{16,18},{32,34},{48,50},{64,66},{80,82},{96,98},{112,114}} | collective-permute-start | bytes 491528 | tf_op jit(solution)/shard_map/ppermute | solution.py:90
  286.0 10.3 %collective-permute-start.13 = (f32[80,512]{1,0:T(8,128)S(1)}, f32[80,512]{1,0:T(8,128)S(1)}, u32[]{:S(2)}, u32[]{:S(2)}) collective-permute-start(f32[80,512]{1,0:T(8,128)S(1)} %get-tuple-element.21), channel_id=1, source_target_pairs={{0,14},{16,30},{32,46},{48,62},{64,78},{80,94},{96,110},{112,126}} | collective-permute-start | bytes 491528 | tf_op jit(solution)/shard_map/ppermute | solution.py:90
  287.3 11.2 %collective-permute-start.14 = (f32[80,512]{1,0:T(8,128)S(1)}, f32[80,512]{1,0:T(8,128)S(1)}, u32[]{:S(2)}, u32[]{:S(2)}) collective-permute-start(f32[80,512]{1,0:T(8,128)S(1)} %get-tuple-element.20), channel_id=1, source_target_pairs={{0,15},{16,31},{32,47},{48,63},{64,79},{80,95},{96,111},{112,127}} | collective-permute-start | bytes 491528 | tf_op jit(solution)/shard_map/ppermute | solution.py:90
  288.7 11.8 %collective-permute-start.2 = (f32[80,512]{1,0:T(8,128)S(1)}, f32[80,512]{1,0:T(8,128)S(1)}, u32[]{:S(2)}, u32[]{:S(2)}) collective-permute-start(f32[80,512]{1,0:T(8,128)S(1)} %get-tuple-element.32), channel_id=1, source_target_pairs={{0,3},{16,19},{32,35},{48,51},{64,67},{80,83},{96,99},{112,115}} | collective-permute-start | bytes 491528 | tf_op jit(solution)/shard_map/ppermute | solution.py:90
  290.0 12.5 %collective-permute-start.3 = (f32[80,512]{1,0:T(8,128)S(1)}, f32[80,512]{1,0:T(8,128)S(1)}, u32[]{:S(2)}, u32[]{:S(2)}) collective-permute-start(f32[80,512]{1,0:T(8,128)S(1)} %get-tuple-element.31), channel_id=1, source_target_pairs={{0,4},{16,20},{32,36},{48,52},{64,68},{80,84},{96,100},{112,116}} | collective-permute-start | bytes 491528 | tf_op jit(solution)/shard_map/ppermute | solution.py:90
  292.8 11.8 %collective-permute-start.4 = (f32[80,512]{1,0:T(8,128)S(1)}, f32[80,512]{1,0:T(8,128)S(1)}, u32[]{:S(2)}, u32[]{:S(2)}) collective-permute-start(f32[80,512]{1,0:T(8,128)S(1)} %get-tuple-element.30), channel_id=1, source_target_pairs={{0,5},{16,21},{32,37},{48,53},{64,69},{80,85},{96,101},{112,117}} | collective-permute-start | bytes 491528 | tf_op jit(solution)/shard_map/ppermute | solution.py:90
  296.3 10.3 %collective-permute-start.5 = (f32[80,512]{1,0:T(8,128)S(1)}, f32[80,512]{1,0:T(8,128)}, u32[]{:S(2)}, u32[]{:S(2)}) collective-permute-start(f32[80,512]{1,0:T(8,128)S(1)} %get-tuple-element.29), channel_id=1, source_target_pairs={{0,6},{16,22},{32,38},{48,54},{64,70},{80,86},{96,102},{112,118}} | collective-permute-start | bytes 491528 | tf_op jit(solution)/shard_map/ppermute | solution.py:90
  300.5 9.4 %collective-permute-start.7 = (f32[80,512]{1,0:T(8,128)S(1)}, f32[80,512]{1,0:T(8,128)}, u32[]{:S(2)}, u32[]{:S(2)}) collective-permute-start(f32[80,512]{1,0:T(8,128)S(1)} %get-tuple-element.27), channel_id=1, source_target_pairs={{0,8},{16,24},{32,40},{48,56},{64,72},{80,88},{96,104},{112,120}} | collective-permute-start | bytes 491528 | tf_op jit(solution)/shard_map/ppermute | solution.py:90
  302.4 11.0 %collective-permute-start.8 = (f32[80,512]{1,0:T(8,128)S(1)}, f32[80,512]{1,0:T(8,128)}, u32[]{:S(2)}, u32[]{:S(2)}) collective-permute-start(f32[80,512]{1,0:T(8,128)S(1)} %get-tuple-element.26), channel_id=1, source_target_pairs={{0,9},{16,25},{32,41},{48,57},{64,73},{80,89},{96,105},{112,121}} | collective-permute-start | bytes 491528 | tf_op jit(solution)/shard_map/ppermute | solution.py:90
  304.6 11.1 %collective-permute-start.9 = (f32[80,512]{1,0:T(8,128)S(1)}, f32[80,512]{1,0:T(8,128)}, u32[]{:S(2)}, u32[]{:S(2)}) collective-permute-start(f32[80,512]{1,0:T(8,128)S(1)} %get-tuple-element.25), channel_id=1, source_target_pairs={{0,10},{16,26},{32,42},{48,58},{64,74},{80,90},{96,106},{112,122}} | collective-permute-start | bytes 491528 | tf_op jit(solution)/shard_map/ppermute | solution.py:90
  318.8 23.2 %collective-permute-start.15 = (f32[80,512]{1,0:T(8,128)S(1)}, f32[80,512]{1,0:T(8,128)S(1)}, u32[]{:S(2)}, u32[]{:S(2)}) collective-permute-start(f32[80,512]{1,0:T(8,128)S(1)} %fusion.16), channel_id=1, source_target_pairs={{0,1},{1,2},{2,3},{3,4},{4,5},{5,6},{6,7},{7,8},{8,9},{9,10},{10,1... | collective-permute-start | bytes 491528 | tf_op jit(solution)/shard_map/ppermute | solution.py:106
  320.6 21.6 %collective-permute-start.23 = (f32[80,512]{1,0:T(8,128)S(1)}, f32[80,512]{1,0:T(8,128)S(1)}, u32[]{:S(2)}, u32[]{:S(2)}) collective-permute-start(f32[80,512]{1,0:T(8,128)S(1)} %fusion.16), channel_id=1, source_target_pairs={{1,0},{2,1},{3,2},{4,3},{5,4},{6,5},{7,6},{8,7},{9,8},{10,9},{11,1... | collective-permute-start | bytes 491528 | tf_op jit(solution)/shard_map/ppermute | solution.py:108
  324.2 12.0 %collective-permute-start.31 = (f32[80,512]{1,0:T(8,128)S(1)}, f32[80,512]{1,0:T(8,128)S(1)}, u32[]{:S(2)}, u32[]{:S(2)}) collective-permute-start(f32[80,512]{1,0:T(8,128)S(1)} %collective-permute-done.30), channel_id=1, source_target_pairs={{0,16},{16,32},{32,48},{48,64},{64,80},{80,96},{96,112},{112,0},{1... | collective-permute-start | bytes 491528 | tf_op jit(solution)/shard_map/ppermute | solution.py:123
  327.9 14.2 %collective-permute-start.32 = (f32[80,512]{1,0:T(8,128)S(1)}, f32[80,512]{1,0:T(8,128)S(1)}, u32[]{:S(2)}, u32[]{:S(2)}) collective-permute-start(f32[80,512]{1,0:T(8,128)S(1)} %collective-permute-done.30), channel_id=1, source_target_pairs={{0,32},{16,48},{32,64},{48,80},{64,96},{80,112},{96,0},{112,16},{1... | collective-permute-start | bytes 491528 | tf_op jit(solution)/shard_map/ppermute | solution.py:123
  336.2 10.9 %collective-permute-start.33 = (f32[80,512]{1,0:T(8,128)S(1)}, f32[80,512]{1,0:T(8,128)S(1)}, u32[]{:S(2)}, u32[]{:S(2)}) collective-permute-start(f32[80,512]{1,0:T(8,128)S(1)} %collective-permute-done.30), channel_id=1, source_target_pairs={{0,48},{16,64},{32,80},{48,96},{64,112},{80,0},{96,16},{112,32},{1... | collective-permute-start | bytes 491528 | tf_op jit(solution)/shard_map/ppermute | solution.py:123
  336.3 16.2 %collective-permute-start.34 = (f32[80,512]{1,0:T(8,128)S(1)}, f32[80,512]{1,0:T(8,128)S(1)}, u32[]{:S(2)}, u32[]{:S(2)}) collective-permute-start(f32[80,512]{1,0:T(8,128)S(1)} %collective-permute-done.30), channel_id=1, source_target_pairs={{0,64},{16,80},{32,96},{48,112},{64,0},{80,16},{96,32},{112,48},{1... | collective-permute-start | bytes 491528 | tf_op jit(solution)/shard_map/ppermute | solution.py:123
  342.0 28.6 %collective-permute-start.35 = (f32[80,512]{1,0:T(8,128)S(1)}, f32[80,512]{1,0:T(8,128)S(1)}, u32[]{:S(2)}, u32[]{:S(2)}) collective-permute-start(f32[80,512]{1,0:T(8,128)S(1)} %collective-permute-done.30), channel_id=1, source_target_pairs={{0,80},{16,96},{32,112},{48,0},{64,16},{80,32},{96,48},{112,64},{1... | collective-permute-start | bytes 491528 | tf_op jit(solution)/shard_map/ppermute | solution.py:123
  342.1 10.4 %collective-permute-start.16 = (f32[80,512]{1,0:T(8,128)S(1)}, f32[80,512]{1,0:T(8,128)S(1)}, u32[]{:S(2)}, u32[]{:S(2)}) collective-permute-start(f32[80,512]{1,0:T(8,128)S(1)} %collective-permute-done.15), channel_id=1, source_target_pairs={{0,1},{1,2},{2,3},{3,4},{4,5},{5,6},{6,7},{7,8},{8,9},{9,10},{10,1... | collective-permute-start | bytes 491528 | tf_op jit(solution)/shard_map/ppermute | solution.py:106
  342.2 37.0 %collective-permute-start.36 = (f32[80,512]{1,0:T(8,128)S(1)}, f32[80,512]{1,0:T(8,128)S(1)}, u32[]{:S(2)}, u32[]{:S(2)}) collective-permute-start(f32[80,512]{1,0:T(8,128)S(1)} %collective-permute-done.30), channel_id=1, source_target_pairs={{0,96},{16,112},{32,0},{48,16},{64,32},{80,48},{96,64},{112,80},{1... | collective-permute-start | bytes 491528 | tf_op jit(solution)/shard_map/ppermute | solution.py:123
  352.5 9.5 %collective-permute-start.17 = (f32[80,512]{1,0:T(8,128)S(1)}, f32[80,512]{1,0:T(8,128)S(1)}, u32[]{:S(2)}, u32[]{:S(2)}) collective-permute-start(f32[80,512]{1,0:T(8,128)S(1)} %collective-permute-done.16), channel_id=1, source_target_pairs={{0,1},{1,2},{2,3},{3,4},{4,5},{5,6},{6,7},{7,8},{8,9},{9,10},{10,1... | collective-permute-start | bytes 491528 | tf_op jit(solution)/shard_map/ppermute | solution.py:106
  352.5 35.5 %collective-permute-start.37 = (f32[80,512]{1,0:T(8,128)S(1)}, f32[80,512]{1,0:T(8,128)S(1)}, u32[]{:S(2)}, u32[]{:S(2)}) collective-permute-start(f32[80,512]{1,0:T(8,128)S(1)} %collective-permute-done.30), channel_id=1, source_target_pairs={{0,112},{16,0},{32,16},{48,32},{64,48},{80,64},{96,80},{112,96},{1... | collective-permute-start | bytes 491528 | tf_op jit(solution)/shard_map/ppermute | solution.py:123
  353.5 17.1 %collective-permute-start.25 = (f32[80,512]{1,0:T(8,128)S(1)}, f32[80,512]{1,0:T(8,128)S(1)}, u32[]{:S(2)}, u32[]{:S(2)}) collective-permute-start(f32[80,512]{1,0:T(8,128)S(1)} %collective-permute-done.24), channel_id=1, source_target_pairs={{1,0},{2,1},{3,2},{4,3},{5,4},{6,5},{7,6},{8,7},{9,8},{10,9},{11,1... | collective-permute-start | bytes 491528 | tf_op jit(solution)/shard_map/ppermute | solution.py:108
  361.9 8.6 %collective-permute-start.18 = (f32[80,512]{1,0:T(8,128)S(1)}, f32[80,512]{1,0:T(8,128)S(1)}, u32[]{:S(2)}, u32[]{:S(2)}) collective-permute-start(f32[80,512]{1,0:T(8,128)S(1)} %collective-permute-done.17), channel_id=1, source_target_pairs={{0,1},{1,2},{2,3},{3,4},{4,5},{5,6},{6,7},{7,8},{8,9},{9,10},{10,1... | collective-permute-start | bytes 491528 | tf_op jit(solution)/shard_map/ppermute | solution.py:106
  370.6 8.6 %collective-permute-start.19 = (f32[80,512]{1,0:T(8,128)S(1)}, f32[80,512]{1,0:T(8,128)S(1)}, u32[]{:S(2)}, u32[]{:S(2)}) collective-permute-start(f32[80,512]{1,0:T(8,128)S(1)} %collective-permute-done.18), channel_id=1, source_target_pairs={{0,1},{1,2},{2,3},{3,4},{4,5},{5,6},{6,7},{7,8},{8,9},{9,10},{10,1... | collective-permute-start | bytes 491528 | tf_op jit(solution)/shard_map/ppermute | solution.py:106
  379.2 8.7 %collective-permute-start.20 = (f32[80,512]{1,0:T(8,128)S(1)}, f32[80,512]{1,0:T(8,128)}, u32[]{:S(2)}, u32[]{:S(2)}) collective-permute-start(f32[80,512]{1,0:T(8,128)S(1)} %collective-permute-done.19), channel_id=1, source_target_pairs={{0,1},{1,2},{2,3},{3,4},{4,5},{5,6},{6,7},{7,8},{8,9},{9,10},{10,1... | collective-permute-start | bytes 491528 | tf_op jit(solution)/shard_map/ppermute | solution.py:106
  379.3 10.4 %collective-permute-start.27 = (f32[80,512]{1,0:T(8,128)}, f32[80,512]{1,0:T(8,128)}, u32[]{:S(2)}, u32[]{:S(2)}) collective-permute-start(f32[80,512]{1,0:T(8,128)} %collective-permute-done.26), channel_id=1, source_target_pairs={{1,0},{2,1},{3,2},{4,3},{5,4},{6,5},{7,6},{8,7},{9,8},{10,9},{11,1... | collective-permute-start | bytes 491528 | tf_op jit(solution)/shard_map/ppermute | solution.py:108
  388.0 9.0 %collective-permute-start.21 = (f32[80,512]{1,0:T(8,128)}, f32[80,512]{1,0:T(8,128)}, u32[]{:S(2)}, u32[]{:S(2)}) collective-permute-start(f32[80,512]{1,0:T(8,128)} %collective-permute-done.20), channel_id=1, source_target_pairs={{0,1},{1,2},{2,3},{3,4},{4,5},{5,6},{6,7},{7,8},{8,9},{9,10},{10,1... | collective-permute-start | bytes 491528 | tf_op jit(solution)/shard_map/ppermute | solution.py:106
  389.7 8.8 %collective-permute-start.28 = (f32[80,512]{1,0:T(8,128)}, f32[80,512]{1,0:T(8,128)S(1)}, u32[]{:S(2)}, u32[]{:S(2)}) collective-permute-start(f32[80,512]{1,0:T(8,128)} %collective-permute-done.27), channel_id=1, source_target_pairs={{1,0},{2,1},{3,2},{4,3},{5,4},{6,5},{7,6},{8,7},{9,8},{10,9},{11,1... | collective-permute-start | bytes 491528 | tf_op jit(solution)/shard_map/ppermute | solution.py:108
  396.9 8.8 %collective-permute-start.22 = (f32[80,512]{1,0:T(8,128)}, f32[80,512]{1,0:T(8,128)S(1)}, u32[]{:S(2)}, u32[]{:S(2)}) collective-permute-start(f32[80,512]{1,0:T(8,128)} %collective-permute-done.21), channel_id=1, source_target_pairs={{0,1},{1,2},{2,3},{3,4},{4,5},{5,6},{6,7},{7,8},{8,9},{9,10},{10,1... | collective-permute-start | bytes 491528 | tf_op jit(solution)/shard_map/ppermute | solution.py:106
  398.5 21.1 %collective-permute-start.29 = (f32[80,512]{1,0:T(8,128)S(1)}, f32[80,512]{1,0:T(8,128)S(1)}, u32[]{:S(2)}, u32[]{:S(2)}) collective-permute-start(f32[80,512]{1,0:T(8,128)S(1)} %collective-permute-done.28), channel_id=1, source_target_pairs={{1,0},{2,1},{3,2},{4,3},{5,4},{6,5},{7,6},{8,7},{9,8},{10,9},{11,1... | collective-permute-start | bytes 491528 | tf_op jit(solution)/shard_map/ppermute | solution.py:108
  (15 other events, 452.9 us)
